TPU v7x, 256 devices: a whole 4x4x8 slice. The times are simulated.
256 devices in a mesh: seq: 32 (over x, z), head: 8 (over y, core).
Axes of the slice: x: 4, y: 4, z: 8, core: 2. Of those that a mesh axis runs over, the one named last changes fastest.
Arguments:
- att_query: bfloat16 [8192, 16, 128], P('seq', 'head'), may hold values from -9 to 9
- att_key: bfloat16 [8192, 16, 128], P('seq', 'head'), may hold values from -9 to 9
- att_value: bfloat16 [8192, 16, 128], P('seq', 'head'), may hold values from -6 to 6
- norm_gain: float32 [16, 128], P('head'), may hold values from 0.1 to 1.9
- dn_query: bfloat16 [8192, 16, 128], P('seq', 'head'), may hold values from -6 to 6
- dn_key: bfloat16 [8192, 16, 128], P('seq', 'head'), may hold values from -4 to 4
- write_rate: float32 [8192, 16], P('seq', 'head'), may hold values from 0.04 to 0.9
- log_decay: float32 [8192, 16], P('seq', 'head'), may hold values from -1 to 0
- out_grad: bfloat16 [8192, 16, 128], P('seq', 'head'), may hold values from -6 to 6
Outputs:
- block_out: bfloat16 [8192, 16, 128], P('seq', 'head')
- att_query_grad: bfloat16 [8192, 16, 128], P('seq', 'head')
- att_key_grad: bfloat16 [8192, 16, 128], P('seq', 'head')
- att_value_grad: bfloat16 [8192, 16, 128], P('seq', 'head')
- gain_grad: float32 [16, 128], P('head')
- dn_query_grad: bfloat16 [8192, 16, 128], P('seq', 'head')
- dn_key_grad: bfloat16 [8192, 16, 128], P('seq', 'head')
- rate_grad: float32 [8192, 16], P('seq', 'head')
- decay_grad: float32 [8192, 16], P('seq', 'head')
All inputs are finite; a program needn't handle non-finite values.
Results may differ from a plain program's by a relative error of at most 0.018.
Values may be sent and summed in bfloat16 or wider, within the bound.
No kernel may reach another device: no remote copies, remote signals or barrier semaphores. Data moves between devices by JAX's collectives and lax.ppermute only.
A program may use at most 64 MiB of HBM per device.

v0:
```python
import jax
import jax.numpy as jnp
from jax import lax
from jax.sharding import PartitionSpec as P

WIN = 1024
CH = 64


MATMUL_ACCURACY = lax.Precision.HIGHEST
EPSILON = 1e-06


def shifted_2(block, axis, distance):
    devices = range(lax.axis_size(axis))
    route = [(i - distance, i) for i in devices if i - distance in devices]
    return lax.ppermute(block, axis, route)


def unit_rows(matrix):
    return matrix * lax.rsqrt(jnp.sum(matrix * matrix, axis=-1, keepdims=True) + EPSILON)


def delta_block(memory_state, pieces):
    query_vectors, key_vectors, value_rows, rate_rows, decay_rows = pieces
    length = key_vectors.shape[1]
    lower = jnp.tril(jnp.ones((length, length), jnp.float32))
    strict = lower - jnp.eye(length, dtype=jnp.float32)
    running_state = jnp.cumsum(decay_rows, axis=1)
    ratio = jnp.exp((running_state[:, :, None] - running_state[:, None, :]) * lower) * lower
    state_increment = jnp.exp(running_state)
    intersection = jnp.einsum("htk,hsk->hts", key_vectors, key_vectors, precision=MATMUL_ACCURACY)
    system = (
        jnp.eye(length, dtype=jnp.float32) + rate_rows[:, :, None] * ratio * strict * intersection
    )
    retrieved_values = jnp.einsum(
        "nex,nxp->nep", key_vectors, memory_state, precision=MATMUL_ACCURACY
    )
    target = rate_rows[:, :, None] * (value_rows - state_increment[:, :, None] * retrieved_values)
    newest_state = jax.scipy.linalg.solve_triangular(system, target, lower=True, unit_diagonal=True)
    local_scores = (
        jnp.einsum("htk,hsk->hts", query_vectors, key_vectors, precision=MATMUL_ACCURACY) * ratio
    )
    state_output = state_increment[:, :, None] * jnp.einsum(
        "nex,nxp->nep", query_vectors, memory_state, precision=MATMUL_ACCURACY
    )
    state_output = state_output + jnp.einsum(
        "hts,hsv->htv", local_scores, newest_state, precision=MATMUL_ACCURACY
    )
    retained_state = jnp.exp(running_state[:, -1:] - running_state)
    memory_state = jnp.exp(running_state[:, -1])[:, None, None] * memory_state + jnp.einsum(
        "wpa,wpn->wan",
        key_vectors * retained_state[:, :, None],
        newest_state,
        precision=MATMUL_ACCURACY,
    )
    return (memory_state, state_output)


def delta_sweep(memory_state, query_vectors, key_vectors, value_rows, rate_rows, decay_rows):
    head_count, length = (key_vectors.shape[0], key_vectors.shape[1])
    blocks = length // CH

    def cut_blocks(array):
        return jnp.moveaxis(array.reshape((head_count, blocks, CH) + array.shape[2:]), 1, 0)

    last_state, state_output = lax.scan(
        delta_block,
        memory_state,
        (
            cut_blocks(query_vectors),
            cut_blocks(key_vectors),
            cut_blocks(value_rows),
            cut_blocks(rate_rows),
            cut_blocks(decay_rows),
        ),
    )
    return (
        last_state,
        jnp.moveaxis(state_output, 0, 1).reshape(head_count, length, state_output.shape[-1]),
    )


def window_softmax(rows_here, keys_here, values_here, alive_keys):
    block_rows = rows_here.shape[0]
    span_rows = keys_here.shape[0]
    reach_back = span_rows - block_rows
    scores = jnp.einsum("qhd,khd->hqk", rows_here, keys_here) * rows_here.shape[-1] ** (-0.5)
    query_pos = jnp.arange(block_rows, dtype=jnp.int32)[:, None]
    key_pos = jnp.arange(span_rows, dtype=jnp.int32)[None, :]
    allowed = (key_pos > query_pos) & (key_pos <= query_pos + reach_back) & alive_keys[None, :]
    scores = jnp.where(allowed[None], scores, -1e30)
    shifted = jnp.exp(scores - jnp.max(scores, axis=-1, keepdims=True))
    weights_bf = (shifted / jnp.sum(shifted, axis=-1, keepdims=True)).astype(jnp.bfloat16)
    return jnp.einsum("hqk,khd->qhd", weights_bf.astype(jnp.float32), values_here)


def attend(query_vectors, key_vectors, value_rows, alive_keys):
    outputs = [window_softmax(query_vectors, key_vectors, value_rows, alive_keys)]
    return jnp.concatenate(outputs, axis=0)


def apply_map(matrix, operand):
    return jnp.einsum("hij,hjv->hiv", matrix, operand, precision=MATMUL_ACCURACY)


def body(
    att_query, att_key, att_value, norm_gain, dn_query, dn_key, write_rate, log_decay, out_grad
):
    row_count, head_count, head_width = att_query.shape
    rim_rows = min(WIN, row_count)
    reach_back = max(1, WIN // row_count)
    my_shard = lax.axis_index("seq")
    shard_count = lax.axis_size("seq")
    older_keys = []
    older_values = []
    for offset in range(reach_back):
        came_key, came_value = shifted_2((att_key, att_value), "seq", offset + 1)
        older_keys.insert(0, came_key)
        older_values.insert(0, came_value)
    all_keys = jnp.concatenate(older_keys + [att_key], axis=0).astype(jnp.float32)
    all_values = jnp.concatenate(older_values + [att_value], axis=0).astype(jnp.float32)
    alive_keys = my_shard * row_count - WIN + jnp.arange(WIN + row_count, dtype=jnp.int32) >= 0

    def attention_core(query_vectors, key_vectors, value_rows):
        return attend(query_vectors, key_vectors, value_rows, alive_keys)

    attended, attention_pull = jax.vjp(
        attention_core, att_query.astype(jnp.float32), all_keys, all_values
    )
    square_part = jnp.sum(attended * attended, axis=(1, 2))
    square_all = lax.psum(square_part, "head")
    features = head_count * lax.axis_size("head") * head_width
    inverse = lax.rsqrt(square_all / features + EPSILON)
    scaled = attended * inverse[:, None, None]
    values = (scaled * norm_gain[None]).astype(jnp.bfloat16)
    query_heads = jnp.swapaxes(dn_query, 0, 1).astype(jnp.float32)
    key_heads = jnp.swapaxes(dn_key, 0, 1).astype(jnp.float32)
    value_heads = jnp.swapaxes(values, 0, 1)
    rate_heads = write_rate.T
    decay_heads = log_decay.T
    identity = jnp.broadcast_to(
        jnp.eye(head_width, dtype=jnp.float32), (head_count, head_width, head_width)
    )
    seed_state = jnp.concatenate(
        [identity, jnp.zeros((head_count, head_width, head_width), jnp.float32)], axis=-1
    )
    folded_values = jnp.concatenate(
        [jnp.zeros(value_heads.shape, jnp.float32), value_heads.astype(jnp.float32)], axis=-1
    )
    summary, unused_out = delta_sweep(
        seed_state,
        unit_rows(query_heads),
        unit_rows(key_heads),
        folded_values,
        rate_heads,
        decay_heads,
    )
    carry_map = summary[..., :head_width]
    carry_add = summary[..., head_width:]
    empty_state = jnp.zeros_like(carry_add)

    def relay(turn, current):
        return shifted_2(apply_map(carry_map, current) + carry_add, "seq", 1)

    start_state = lax.fori_loop(0, shard_count - 1, relay, empty_state)

    def local_delta(start_in, query_in, key_in, value_in, rate_in, decay_in):
        last_state, state_output = delta_sweep(
            start_in,
            unit_rows(query_in),
            unit_rows(key_in),
            value_in.astype(jnp.float32),
            rate_in,
            decay_in,
        )
        return (state_output, last_state)

    (state_output, last_state), delta_pull = jax.vjp(
        local_delta, start_state, query_heads, key_heads, value_heads, rate_heads, decay_heads
    )
    cotangent = jnp.swapaxes(out_grad, 0, 1).astype(jnp.float32)
    own_back = delta_pull((cotangent, empty_state))[0]
    flipped = jnp.swapaxes(carry_map, 1, 2)

    def relay_back(turn, current):
        return shifted_2(apply_map(flipped, current) + own_back, "seq", -1)

    later_grad = lax.fori_loop(0, shard_count - 1, relay_back, empty_state)
    delta_grads = delta_pull((cotangent, later_grad))
    value_grad = jnp.swapaxes(delta_grads[3], 0, 1).astype(jnp.float32)
    weighted = value_grad * norm_gain[None]
    dot_part = jnp.sum(weighted * attended, axis=(1, 2))
    gain_part = jnp.sum(value_grad * scaled, axis=0)
    dot_all = lax.psum(dot_part, "head")
    gain_grad = lax.psum(gain_part, "seq")
    attended_grad = (
        inverse[:, None, None] * weighted
        - attended * (inverse * inverse * inverse * dot_all / features)[:, None, None]
    )
    query_grad, keys_grad, values_grad = attention_pull(attended_grad)
    own_key_grad = keys_grad[WIN:]
    own_value_grad = values_grad[WIN:]
    extra_key = jnp.zeros((rim_rows, head_count, head_width), jnp.float32)
    extra_value = jnp.zeros((rim_rows, head_count, head_width), jnp.float32)
    for offset in range(reach_back):
        segment = reach_back - 1 - offset
        sent_key = keys_grad[segment * rim_rows : (segment + 1) * rim_rows]
        sent_value = values_grad[segment * rim_rows : (segment + 1) * rim_rows]
        came_key, came_value = (
            shifted_2(sent_key.astype(jnp.bfloat16), "seq", -(offset + 1)).astype(sent_key.dtype),
            shifted_2(sent_value.astype(jnp.bfloat16), "seq", -(offset + 1)).astype(
                sent_value.dtype
            ),
        )
        extra_key = extra_key + came_key
        extra_value = extra_value + came_value
    own_key_grad = own_key_grad.at[row_count - rim_rows :].add(extra_key)
    own_value_grad = own_value_grad.at[row_count - rim_rows :].add(extra_value)
    block_out = jnp.swapaxes(state_output, 0, 1).astype(jnp.bfloat16)
    return (
        block_out,
        query_grad.astype(jnp.bfloat16),
        own_key_grad.astype(jnp.bfloat16),
        own_value_grad.astype(jnp.bfloat16),
        gain_grad,
        jnp.swapaxes(delta_grads[1], 0, 1).astype(jnp.bfloat16),
        jnp.swapaxes(delta_grads[2], 0, 1).astype(jnp.bfloat16),
        delta_grads[4].T,
        delta_grads[5].T,
    )


def solution(mesh):
    return jax.shard_map(
        body,
        mesh=mesh,
        in_specs=(
            P("seq", "head", None),
            P("seq", "head", None),
            P("seq", "head", None),
            P("head", None),
            P("seq", "head", None),
            P("seq", "head", None),
            P("seq", "head"),
            P("seq", "head"),
            P("seq", "head", None),
        ),
        out_specs=(
            P("seq", "head", None),
            P("seq", "head", None),
            P("seq", "head", None),
            P("seq", "head", None),
            P("head", None),
            P("seq", "head", None),
            P("seq", "head", None),
            P("seq", "head"),
            P("seq", "head"),
        ),
        check_vma=False,
    )
```

profile of v0, /device:TPU:162, one launch (start us, length us, event | category | flops | bytes accessed | tf_op | source)
XLA Modules:
  0.0 1278.0 jit_solution(2413856035602274087)
XLA Ops:
  4.2 7.7 collective-permute-start.7
  50.1 6.8 collective-permute-done.4
  59.0 14.4 %psum.21 = f32[256]{0:T(256)S(1)} all-reduce(f32[256]{0:T(256)S(1)} %get-tuple-element.2481), channel_id=1, replica_groups=mesh['seq'=32,'head'=8] {'head'}, use_global_device_ids=true, to_apply=%region_4.5 | all-reduce | flops 256 | bytes 2048 | tf_op jit(solution)/shard_map/psum | solution.py:132
  78.7 69.7 %while.136 = (s32[]{:T(128)}, f32[2,128,256]{2,1,0:T(8,128)S(1)}, f32[4,2,64]{2,1,0:T(2,128)}, f32[4,2,64,128]{3,2,1,0:T(8,128)S(1)}, f32[4,2,64]{2,1,0:T(2,128)...) while((s32[]{:T(128)}, f32[2,128,256]{2,1,0:T(8,128)S(1)}, f32[4,2,64]{2,1,0:T(2,128)}, ...), condition=%wide.region_7.8_spmd, body=%wide.region_5.0_spmd.sunk | while | flops 138780736 | bytes 1925833 | solution.py:67
  82.6 11.2 custom-call.55
  100.0 11.2 custom-call.55
  117.4 11.2 custom-call.55
  134.9 11.2 custom-call.55
  152.2 311.7 %while.137 = (s32[]{:T(128)}, f32[2,128,128]{2,1,0:T(8,128)S(1)}, f32[2,128,128]{2,1,0:T(8,128)S(1)}, f32[2,128,128]{2,1,0:T(8,128)S(1)}, s32[]{:T(128)}) while((s32[]{:T(128)}, f32[2,128,128]{2,1,0:T(8,128)S(1)}, f32[2,128,128]{2,1,0:T(8,128)S(1)}, f32[2,128,128]{2,1,0:T(8,128)S(1)}, s32[]{:T(128)}) %tuple.298), condition=%wide.region_9.10_spmd, body=%wide.region_8.9_spmd.sunk | while | flops 50364416 | bytes 1048677 | solution.py:166
  290.1 6.9 collective-permute-start
  372.8 6.6 collective-permute-start
  467.6 105.8 %while.139 = (s32[]{:T(128)}, f32[2,128,128]{2,1,0:T(8,128)S(1)}, bf16[4,2,64,128]{3,2,1,0:T(8,128)(2,1)}, f32[4,2,64,64]{3,2,1,0:T(8,128)}, f32[4,2,64]{2,1,0:T...) while((s32[]{:T(128)}, f32[2,128,128]{2,1,0:T(8,128)S(1)}, ...), condition=%wide.region_13.14_spmd.clone.clone, body=%wide.region_11.13_spmd.clone.clone.sunk | while | flops 126304576 | bytes 3452789 | solution.py:67
  472.0 10.6 custom-call.56
  498.4 10.6 custom-call.56
  524.8 10.6 custom-call.56
  551.3 10.6 custom-call.56
  574.0 65.0 %while.141 = (s32[]{:T(128)}, f32[2,128,128]{2,1,0:T(8,128)S(1)}, f32[4,2,1,1]{1,3,2,0:T(1,128)}, f32[4,2,64,128]{3,2,1,0:T(8,128)}, f32[4,2,64,1]{2,1,3,0:T(2,1...) while((s32[]{:T(128)}, f32[2,128,128]{2,1,0:T(8,128)S(1)}, ...), condition=%wide.region_15.17_spmd.clone, body=%wide.region_14.16_spmd.clone.sunk | while | flops 100937792 | bytes 1587911 | solution.py:67
  577.7 9.8 custom-call.59
  594.0 9.8 custom-call.59
  610.2 9.8 custom-call.59
  626.5 9.8 custom-call.59
  639.0 292.8 %while.138 = (s32[]{:T(128)}, f32[2,128,128]{2,1,0:T(8,128)S(1)}, f32[2,128,128]{2,1,0:T(8,128)S(1)}, f32[2,128,128]{2,1,0:T(8,128)S(1)}, s32[]{:T(128)}) while((s32[]{:T(128)}, f32[2,128,128]{2,1,0:T(8,128)S(1)}, f32[2,128,128]{2,1,0:T(8,128)S(1)}, f32[2,128,128]{2,1,0:T(8,128)S(1)}, s32[]{:T(128)}) %tuple.319), condition=%wide.region_17.19_spmd, body=%wide.region_16.18_spmd.sunk | while | flops 50364416 | bytes 1048677 | solution.py:189
  641.2 7.4 collective-permute-done.1
  650.8 7.4 collective-permute-done.1
  660.3 7.4 collective-permute-done.1
  670.0 8.5 collective-permute-done.1
  680.7 8.1 collective-permute-done.1
  699.7 6.8 collective-permute-done.1
  708.7 7.0 collective-permute-done.1
  717.9 7.0 collective-permute-done.1
  727.2 7.0 collective-permute-done.1
  736.4 7.6 collective-permute-done.1
  746.3 8.4 collective-permute-done.1
  756.9 7.3 collective-permute-done.1
  775.1 7.0 collective-permute-done.1
  784.4 7.0 collective-permute-done.1
  793.6 7.0 collective-permute-done.1
  802.9 7.2 collective-permute-done.1
  812.3 8.7 collective-permute-done.1
  823.2 7.7 collective-permute-done.1
  841.8 6.8 collective-permute-done.1
  850.8 7.0 collective-permute-done.1
  860.0 7.0 collective-permute-done.1
  869.3 7.0 collective-permute-done.1
  878.5 7.0 collective-permute-done.1
  887.8 7.0 collective-permute-done.1
  897.0 7.0 collective-permute-done.1
  906.2 7.0 collective-permute-done.1
  915.5 7.0 collective-permute-done.1
  924.7 7.0 collective-permute-done.1
  935.1 192.5 %while.140 = (s32[]{:T(128)}, f32[2,128,128]{2,1,0:T(8,128)S(1)}, f32[4,2,64,128]{3,2,1,0:T(8,128)}, f32[4,2,64,128]{3,2,1,0:T(8,128)}, bf16[4,2,64,128]{3,2,0,1...) while((s32[]{:T(128)}, f32[2,128,128]{2,1,0:T(8,128)S(1)}, ...), condition=%wide.region_29.31_spmd.clone.clone, body=%wide.region_18.30_spmd.clone.clone.sunk | while | flops 258761408 | bytes 5408265 | solution.py:67
  939.3 9.8 custom-call.58
  953.5 9.8 custom-call.57
  987.4 9.8 custom-call.58
  1001.6 9.8 custom-call.57
  1035.5 9.8 custom-call.58
  1049.7 9.8 custom-call.57
  1083.6 9.8 custom-call.58
  1097.8 9.8 custom-call.57
  1130.5 12.4 psum.22
  1161.3 13.9 %collective-permute-start.16 = (bf16[256,2,128]{0,2,1:T(8,128)(2,1)S(1)}, bf16[256,2,128]{0,2,1:T(8,128)(2,1)S(1)}, u32[]{:S(2)}, u32[]{:S(2)}) collective-permute-start(bf16[256,2,128]{0,2,1:T(8,128)(2,1)S(1)} %get-tuple-element.2471), channel_id=1, source_target_pairs={{24,0},{32,8},{40,16},{48,24},{56,32},{64,40},{72,48},{80,56},{88,... | collective-permute-start | bytes 393224 | tf_op jit(solution)/shard_map/ppermute | solution.py:17
  1179.9 67.6 %psum.23 = f32[2,128]{1,0:T(2,128)} all-reduce(f32[2,128]{1,0:T(2,128)S(1)} %copy-done.42), channel_id=1, replica_groups=mesh['seq'=32,'head'=8] {'seq'}, use_global_device_ids=true, to_apply=%region_36.38 | all-reduce | flops 256 | bytes 2048 | tf_op jit(solution)/shard_map/psum | solution.py:196
  1253.7 10.1 collective-permute-start.12
  1267.6 8.6 collective-permute-done.13
  (737 shorter events, 708.7 us)
Async XLA Ops:
  1.7 32.5 %collective-permute-start.6 = (bf16[256,2,128]{2,0,1:T(8,128)(2,1)S(1)}, bf16[256,2,128]{2,0,1:T(8,128)(2,1)S(1)}, u32[]{:S(2)}, u32[]{:S(2)}) collective-permute-start(bf16[256,2,128]{2,0,1:T(8,128)(2,1)S(1)} %copy.247), channel_id=1, source_target_pairs={{0,32},{8,40},{16,48},{24,56},{32,64},{40,72},{48,80},{56,88},{64,... | collective-permute-start | bytes 393224 | tf_op jit(solution)/shard_map/ppermute | solution.py:17
  4.2 36.0 %collective-permute-start.7 = (bf16[256,2,128]{2,0,1:T(8,128)(2,1)S(1)}, bf16[256,2,128]{2,0,1:T(8,128)(2,1)S(1)}, u32[]{:S(2)}, u32[]{:S(2)}) collective-permute-start(bf16[256,2,128]{2,0,1:T(8,128)(2,1)S(1)} %copy.247), channel_id=1, source_target_pairs={{0,24},{8,32},{16,40},{24,48},{32,56},{40,64},{48,72},{56,80},{64,... | collective-permute-start | bytes 393224 | tf_op jit(solution)/shard_map/ppermute | solution.py:17
  11.9 30.7 %collective-permute-start.8 = (bf16[256,2,128]{2,0,1:T(8,128)(2,1)S(1)}, bf16[256,2,128]{2,0,1:T(8,128)(2,1)S(1)}, u32[]{:S(2)}, u32[]{:S(2)}) collective-permute-start(bf16[256,2,128]{2,0,1:T(8,128)(2,1)S(1)} %copy.247), channel_id=1, source_target_pairs={{0,16},{8,24},{16,32},{24,40},{32,48},{40,56},{48,64},{56,72},{64,... | collective-permute-start | bytes 393224 | tf_op jit(solution)/shard_map/ppermute | solution.py:17
  15.3 29.8 %collective-permute-start.9 = (bf16[256,2,128]{2,0,1:T(8,128)(2,1)S(1)}, bf16[256,2,128]{2,0,1:T(8,128)(2,1)S(1)}, u32[]{:S(2)}, u32[]{:S(2)}) collective-permute-start(bf16[256,2,128]{2,0,1:T(8,128)(2,1)S(1)} %copy.247), channel_id=1, source_target_pairs={{0,8},{8,16},{16,24},{24,32},{32,40},{40,48},{48,56},{56,64},{64,7... | collective-permute-start | bytes 393224 | tf_op jit(solution)/shard_map/ppermute | solution.py:17
  30.2 17.6 %collective-permute-start.2 = (bf16[256,2,128]{0,2,1:T(8,128)(2,1)S(1)}, bf16[256,2,128]{0,2,1:T(8,128)(2,1)S(1)}, u32[]{:S(2)}, u32[]{:S(2)}) collective-permute-start(bf16[256,2,128]{0,2,1:T(8,128)(2,1)S(1)} %copy.242), channel_id=1, source_target_pairs={{0,32},{8,40},{16,48},{24,56},{32,64},{40,72},{48,80},{56,88},{64,... | collective-permute-start | bytes 393224 | tf_op jit(solution)/shard_map/ppermute | solution.py:17
  34.2 15.9 %collective-permute-start.3 = (bf16[256,2,128]{0,2,1:T(8,128)(2,1)S(1)}, bf16[256,2,128]{0,2,1:T(8,128)(2,1)S(1)}, u32[]{:S(2)}, u32[]{:S(2)}) collective-permute-start(bf16[256,2,128]{0,2,1:T(8,128)(2,1)S(1)} %copy.242), channel_id=1, source_target_pairs={{0,24},{8,32},{16,40},{24,48},{32,56},{40,64},{48,72},{56,80},{64,... | collective-permute-start | bytes 393224 | tf_op jit(solution)/shard_map/ppermute | solution.py:17
  40.2 16.7 %collective-permute-start.4 = (bf16[256,2,128]{0,2,1:T(8,128)(2,1)S(1)}, bf16[256,2,128]{0,2,1:T(8,128)(2,1)S(1)}, u32[]{:S(2)}, u32[]{:S(2)}) collective-permute-start(bf16[256,2,128]{0,2,1:T(8,128)(2,1)S(1)} %copy.242), channel_id=1, source_target_pairs={{0,16},{8,24},{16,32},{24,40},{32,48},{40,56},{48,64},{56,72},{64,... | collective-permute-start | bytes 393224 | tf_op jit(solution)/shard_map/ppermute | solution.py:17
  42.6 15.2 %collective-permute-start.5 = (bf16[256,2,128]{0,2,1:T(8,128)(2,1)S(1)}, bf16[256,2,128]{0,2,1:T(8,128)(2,1)S(1)}, u32[]{:S(2)}, u32[]{:S(2)}) collective-permute-start(bf16[256,2,128]{0,2,1:T(8,128)(2,1)S(1)} %copy.242), channel_id=1, source_target_pairs={{0,8},{8,16},{16,24},{24,32},{32,40},{40,48},{48,56},{56,64},{64,7... | collective-permute-start | bytes 393224 | tf_op jit(solution)/shard_map/ppermute | solution.py:17
  189.0 9.0 collective-permute-start
  198.9 9.5 collective-permute-start
  228.7 9.2 collective-permute-start
  238.9 9.2 collective-permute-start
  249.0 9.2 collective-permute-start
  259.1 9.2 collective-permute-start
  269.2 9.2 collective-permute-start
  279.3 9.9 collective-permute-start
  290.1 10.5 collective-permute-start
  301.6 9.2 collective-permute-start
  311.7 9.2 collective-permute-start
  321.8 9.2 collective-permute-start
  332.0 9.2 collective-permute-start
  342.1 9.2 collective-permute-start
  352.2 9.2 collective-permute-start
  362.2 9.6 collective-permute-start
  372.8 10.6 collective-permute-start
  384.3 9.2 collective-permute-start
  404.3 9.2 collective-permute-start
  414.4 9.2 collective-permute-start
  424.5 9.2 collective-permute-start
  434.6 9.2 collective-permute-start
  444.7 9.2 collective-permute-start
  454.8 9.2 collective-permute-start
  639.2 9.3 collective-permute-start.1
  648.8 9.3 collective-permute-start.1
  658.4 9.4 collective-permute-start.1
  668.0 10.5 collective-permute-start.1
  678.8 10.1 collective-permute-start.1
  706.8 9.0 collective-permute-start.1
  716.0 9.0 collective-permute-start.1
  725.3 9.0 collective-permute-start.1
  734.5 9.6 collective-permute-start.1
  744.3 10.3 collective-permute-start.1
  754.9 9.3 collective-permute-start.1
  773.2 9.0 collective-permute-start.1
  782.4 9.0 collective-permute-start.1
  791.7 9.0 collective-permute-start.1
  800.9 9.2 collective-permute-start.1
  810.4 10.6 collective-permute-start.1
  821.2 9.7 collective-permute-start.1
  858.1 9.0 collective-permute-start.1
  867.3 9.0 collective-permute-start.1
  876.6 9.0 collective-permute-start.1
  895.1 9.0 collective-permute-start.1
  904.3 9.0 collective-permute-start.1
  913.6 9.0 collective-permute-start.1
  922.8 9.0 collective-permute-start.1
  1157.4 93.6 %collective-permute-start.14 = (bf16[256,2,128]{0,2,1:T(8,128)(2,1)S(1)}, bf16[256,2,128]{0,2,1:T(8,128)(2,1)S(1)}, u32[]{:S(2)}, u32[]{:S(2)}) collective-permute-start(bf16[256,2,128]{0,2,1:T(8,128)(2,1)S(1)} %get-tuple-element.2469), channel_id=1, source_target_pairs={{8,0},{16,8},{24,16},{32,24},{40,32},{48,40},{56,48},{64,56},{72,6... | collective-permute-start | bytes 393224 | tf_op jit(solution)/shard_map/ppermute | solution.py:17
  1159.4 94.3 %collective-permute-start.15 = (bf16[256,2,128]{0,2,1:T(8,128)(2,1)S(1)}, bf16[256,2,128]{0,2,1:T(8,128)(2,1)S(1)}, u32[]{:S(2)}, u32[]{:S(2)}) collective-permute-start(bf16[256,2,128]{0,2,1:T(8,128)(2,1)S(1)} %get-tuple-element.2472), channel_id=1, source_target_pairs={{16,0},{24,8},{32,16},{40,24},{48,32},{56,40},{64,48},{72,56},{80,... | collective-permute-start | bytes 393224 | tf_op jit(solution)/shard_map/ppermute | solution.py:17
  1161.3 102.5 %collective-permute-start.16 = (bf16[256,2,128]{0,2,1:T(8,128)(2,1)S(1)}, bf16[256,2,128]{0,2,1:T(8,128)(2,1)S(1)}, u32[]{:S(2)}, u32[]{:S(2)}) collective-permute-start(bf16[256,2,128]{0,2,1:T(8,128)(2,1)S(1)} %get-tuple-element.2471), channel_id=1, source_target_pairs={{24,0},{32,8},{40,16},{48,24},{56,32},{64,40},{72,48},{80,56},{88,... | collective-permute-start | bytes 393224 | tf_op jit(solution)/shard_map/ppermute | solution.py:17
  1175.2 90.5 %collective-permute-start.17 = (bf16[256,2,128]{0,2,1:T(8,128)(2,1)S(1)}, bf16[256,2,128]{0,2,1:T(8,128)(2,1)S(1)}, u32[]{:S(2)}, u32[]{:S(2)}) collective-permute-start(bf16[256,2,128]{0,2,1:T(8,128)(2,1)S(1)} %get-tuple-element.2470), channel_id=1, source_target_pairs={{32,0},{40,8},{48,16},{56,24},{64,32},{72,40},{80,48},{88,56},{96,... | collective-permute-start | bytes 393224 | tf_op jit(solution)/shard_map/ppermute | solution.py:17
  1177.2 90.4 %collective-permute-start.10 = (bf16[256,2,128]{2,0,1:T(8,128)(2,1)S(1)}, bf16[256,2,128]{2,0,1:T(8,128)(2,1)S(1)}, u32[]{:S(2)}, u32[]{:S(2)}) collective-permute-start(bf16[256,2,128]{2,0,1:T(8,128)(2,1)S(1)} %get-tuple-element.2473), channel_id=1, source_target_pairs={{8,0},{16,8},{24,16},{32,24},{40,32},{48,40},{56,48},{64,56},{72,6... | collective-permute-start | bytes 393224 | tf_op jit(solution)/shard_map/ppermute | solution.py:17
  1251.0 16.5 %collective-permute-start.11 = (bf16[256,2,128]{2,0,1:T(8,128)(2,1)S(1)}, bf16[256,2,128]{2,0,1:T(8,128)(2,1)S(1)}, u32[]{:S(2)}, u32[]{:S(2)}) collective-permute-start(bf16[256,2,128]{2,0,1:T(8,128)(2,1)S(1)} %get-tuple-element.2476), channel_id=1, source_target_pairs={{16,0},{24,8},{32,16},{40,24},{48,32},{56,40},{64,48},{72,56},{80,... | collective-permute-start | bytes 393224 | tf_op jit(solution)/shard_map/ppermute | solution.py:17
  1253.7 13.9 %collective-permute-start.12 = (bf16[256,2,128]{2,0,1:T(8,128)(2,1)S(1)}, bf16[256,2,128]{2,0,1:T(8,128)(2,1)S(1)}, u32[]{:S(2)}, u32[]{:S(2)}) collective-permute-start(bf16[256,2,128]{2,0,1:T(8,128)(2,1)S(1)} %get-tuple-element.2475), channel_id=1, source_target_pairs={{24,0},{32,8},{40,16},{48,24},{56,32},{64,40},{72,48},{80,56},{88,... | collective-permute-start | bytes 393224 | tf_op jit(solution)/shard_map/ppermute | solution.py:17
  1263.8 12.4 collective-permute-start.13
  (62 other events, 997.4 us)
where the time goes:
time: 1290 us; the launch traced here: 1280 us
  waiting for transfers between devices  349 us (27%)
  starting transfers between devices  304 us (24%)
  other arithmetic  272 us (21%)
  matrix products  187 us (14%)
  blocking collectives  94.4 us (7%)
  local copies, waits for them, and re-layouts  67.5 us (5%)
    ppermute x78, waiting for transfers between devices, shifted_2(): return lax.ppermute(block, axis, route)  349 us
    ppermute x78, starting transfers between devices, shifted_2(): return lax.ppermute(block, axis, route)  304 us
    another operation x72, other arithmetic, delta_block(): jax.scipy.linalg.solve_triangular(system, target, lower=True, unit_diagon...  217 us
    psum x1, blocking collectives, body(): gain_grad = lax.psum(gain_part, 'seq')  67.6 us
    dot_general x62, matrix products, apply_map(): jnp.einsum('hij,hjv->hiv', matrix, operand, precision=MATMUL_ACCURACY)  37 us
  transfers between devices with their start and end apart: 78, of which 66 were waited for; matrix products, arithmetic and copies ran while one was open for 2% of the time, Pallas kernels for 0%

commit v1 on v0

--- a/solution.py
+++ b/solution.py
@@ -15,6 +15,33 @@
     devices = range(lax.axis_size(axis))
     route = [(i - distance, i) for i in devices if i - distance in devices]
     return lax.ppermute(block, axis, route)
+
+
+def affine_scan(mat, vec, axis, direction):
+    size = lax.axis_size(axis)
+    distance = 1
+    while distance < size:
+        if 2 * distance >= size:
+            came_vec = shifted_2(vec, axis, direction * distance)
+            vec = apply_map(mat, came_vec) + vec
+        else:
+            came_mat, came_vec = shifted_2((mat, vec), axis, direction * distance)
+            vec = apply_map(mat, came_vec) + vec
+            mat = apply_map(mat, came_mat)
+        distance *= 2
+    return vec
+
+
+def butterfly_sum(block, axis):
+    size = lax.axis_size(axis)
+    if size & (size - 1):
+        return lax.psum(block, axis)
+    distance = 1
+    while distance < size:
+        route = [(i, i ^ distance) for i in range(size)]
+        block = block + lax.ppermute(block, axis, route)
+        distance *= 2
+    return block
 
 
 def unit_rows(matrix):
@@ -160,10 +187,7 @@
     carry_add = summary[..., head_width:]
     empty_state = jnp.zeros_like(carry_add)
 
-    def relay(turn, current):
-        return shifted_2(apply_map(carry_map, current) + carry_add, "seq", 1)
-
-    start_state = lax.fori_loop(0, shard_count - 1, relay, empty_state)
+    start_state = shifted_2(affine_scan(carry_map, carry_add, "seq", 1), "seq", 1)
 
     def local_delta(start_in, query_in, key_in, value_in, rate_in, decay_in):
         last_state, state_output = delta_sweep(
@@ -180,20 +204,17 @@
         local_delta, start_state, query_heads, key_heads, value_heads, rate_heads, decay_heads
     )
     cotangent = jnp.swapaxes(out_grad, 0, 1).astype(jnp.float32)
-    own_back = delta_pull((cotangent, empty_state))[0]
+    start_weights = unused_out[..., :head_width]
+    own_back = jnp.einsum("hti,htv->hiv", start_weights, cotangent, precision=MATMUL_ACCURACY)
     flipped = jnp.swapaxes(carry_map, 1, 2)
-
-    def relay_back(turn, current):
-        return shifted_2(apply_map(flipped, current) + own_back, "seq", -1)
-
-    later_grad = lax.fori_loop(0, shard_count - 1, relay_back, empty_state)
+    later_grad = shifted_2(affine_scan(flipped, own_back, "seq", -1), "seq", -1)
     delta_grads = delta_pull((cotangent, later_grad))
     value_grad = jnp.swapaxes(delta_grads[3], 0, 1).astype(jnp.float32)
     weighted = value_grad * norm_gain[None]
     dot_part = jnp.sum(weighted * attended, axis=(1, 2))
     gain_part = jnp.sum(value_grad * scaled, axis=0)
     dot_all = lax.psum(dot_part, "head")
-    gain_grad = lax.psum(gain_part, "seq")
+    gain_grad = butterfly_sum(gain_part, "seq")
     attended_grad = (
         inverse[:, None, None] * weighted
         - attended * (inverse * inverse * inverse * dot_all / features)[:, None, None]

time: 1290 us -> 620 us (0.48)
  waiting for transfers between devices: 349 us -> 39.9 us
  starting transfers between devices: 304 us -> 150 us
  other arithmetic: 272 us -> 181 us
  blocking collectives: 94.4 us -> 26.9 us
  matrix products: 187 us -> 151 us
    ppermute x78 -> x36, waiting for transfers between devices: 349 us -> 26.9 us  [shifted_2(): return lax.ppermute(block, axis, route)]
    ppermute x78 -> x36, starting transfers between devices: 304 us -> 144 us  [shifted_2(): return lax.ppermute(block, axis, route)]
    another operation x72 -> x52, other arithmetic: 217 us -> 131 us  [delta_block(): jax.scipy.linalg.solve_triangular(system, target, lower=True, unit_diagon...]
    psum x1 -> x0, blocking collectives: 67.6 us -> none  [body(): gain_grad = lax.psum(gain_part, 'seq')]
    dot_general x62 -> x18, matrix products: 37 us -> 5.71 us  [apply_map(): jnp.einsum('hij,hjv->hiv', matrix, operand, precision=MATMUL_ACCURACY)]
    ppermute x0 -> x5, waiting for transfers between devices: none -> 13 us  [butterfly_sum(): block = block + lax.ppermute(block, axis, route)]
  transfers between devices with their start and end apart: 78 -> 41, of which waited for: 66 -> 9; matrix products, arithmetic and copies ran while one was open for 2% -> 23% of each run, Pallas kernels for 0% -> 0%
where the time goes in v1:
time: 620 us; the launch traced here: 612 us
  other arithmetic  181 us (29%)
  matrix products  151 us (24%)
  starting transfers between devices  150 us (24%)
  local copies, waits for them, and re-layouts  59.6 us (10%)
  waiting for transfers between devices  39.9 us (6%)
  blocking collectives  26.9 us (4%)
    ppermute x36, starting transfers between devices, shifted_2(): return lax.ppermute(block, axis, route)  144 us
    another operation x52, other arithmetic, delta_block(): jax.scipy.linalg.solve_triangular(system, target, lower=True, unit_diagon...  131 us
    ppermute x36, waiting for transfers between devices, shifted_2(): return lax.ppermute(block, axis, route)  26.9 us
    dot_general x16, matrix products, delta_block(): jnp.einsum('htk,hsk->hts', query_vectors, key_vectors, precision=MATMUL_A...  22.8 us
    dot_general x16, matrix products, delta_block(): jnp.einsum('nex,nxp->nep', query_vectors, memory_state, precision=MATMUL_...  21.8 us
    dot_general x16, matrix products, delta_block(): jnp.einsum('nex,nxp->nep', key_vectors, memory_state, precision=MATMUL_AC...  18.7 us
    dot_general x16, matrix products, delta_block(): jnp.einsum('htk,hsk->hts', key_vectors, key_vectors, precision=MATMUL_ACC...  18.1 us
    dot_general x16, matrix products, delta_block(): jnp.einsum('hts,hsv->htv', local_scores, newest_state, precision=MATMUL_A...  16.9 us
  transfers between devices with their start and end apart: 41, of which 9 were waited for; matrix products, arithmetic and copies ran while one was open for 23% of the time, Pallas kernels for 0%

profile of v1, /device:TPU:162, one launch (start us, length us, event | category | flops | bytes accessed | tf_op | source)
XLA Modules:
  0.0 611.7 jit_solution(2507438472353288977)
XLA Ops:
  1.7 2.5 collective-permute-start.4
  4.2 7.7 %collective-permute-start.5 = (bf16[256,2,128]{2,0,1:T(8,128)(2,1)S(1)}, bf16[256,2,128]{2,0,1:T(8,128)(2,1)S(1)}, u32[]{:S(2)}, u32[]{:S(2)}) collective-permute-start(bf16[256,2,128]{2,0,1:T(8,128)(2,1)S(1)} %copy.256), channel_id=1, source_target_pairs={{0,24},{8,32},{16,40},{24,48},{32,56},{40,64},{48,72},{56,80},{64,... | collective-permute-start | bytes 393224 | tf_op jit(solution)/shard_map/ppermute | solution.py:17
  11.9 3.4 collective-permute-start.6
  15.3 2.9 collective-permute-start.7
  19.3 4.0 collective-permute-start
  34.4 5.9 collective-permute-start.1
  40.4 2.4 collective-permute-start.2
  42.8 2.5 collective-permute-start.3
  49.2 6.8 %collective-permute-done.2 = bf16[256,2,128]{0,2,1:T(8,128)(2,1)S(1)} collective-permute-done((bf16[256,2,128]{0,2,1:T(8,128)(2,1)S(1)}, bf16[256,2,128]{0,2,1:T(8,128)(2,1)S(1)}, u32[]{:S(2)}, u32[]{:S(2)}) %collective-permute-start.2) | collective-permute-done | bytes 131104 | tf_op jit(solution)/shard_map/ppermute | solution.py:17
  55.9 2.2 collective-permute-done.3
  59.0 14.3 %psum.14 = f32[256]{0:T(256)} all-reduce(f32[256]{0:T(256)S(1)} %get-tuple-element.2071), channel_id=1, replica_groups=mesh['seq'=32,'head'=8] {'head'}, use_global_device_ids=true, to_apply=%region_5.6 | all-reduce | flops 256 | bytes 2048 | tf_op jit(solution)/shard_map/psum | solution.py:159
  78.5 84.0 %while.102 = (s32[]{:T(128)}, f32[2,128,256]{2,1,0:T(8,128)S(1)}, f32[4,2,64,256]{3,2,0,1:T(8,128)}, f32[4,2,64]{2,1,0:T(2,128)}, f32[4,2,64,128]{3,2,1,0:T(8,12...) while((s32[]{:T(128)}, f32[2,128,256]{2,1,0:T(8,128)S(1)}, ...), condition=%wide.region_8.9_spmd, body=%wide.region_6.0_spmd.sunk | while | flops 226959424 | bytes 3010777 | solution.py:94
  83.6 10.6 %custom-call.50 = f32[2,1,64,64]{2,3,1,0:T(8,128)S(1)} custom-call(f32[2,1,64,64]{3,2,1,0:T(8,128)} %fusion.383), custom_call_target="InvertDiagBlocksLowerTriangular" | custom-call | tf_op jit(solution)/shard_map/while/body/eval_jaxpr/jit(_solve_triangular)/vmap()/triangular_solve | solution.py:67
  104.6 10.6 %custom-call.50 = f32[2,1,64,64]{2,3,1,0:T(8,128)S(1)} custom-call(f32[2,1,64,64]{3,2,1,0:T(8,128)} %fusion.383), custom_call_target="InvertDiagBlocksLowerTriangular" | custom-call | tf_op jit(solution)/shard_map/while/body/eval_jaxpr/jit(_solve_triangular)/vmap()/triangular_solve | solution.py:67
  125.6 10.6 %custom-call.50 = f32[2,1,64,64]{2,3,1,0:T(8,128)S(1)} custom-call(f32[2,1,64,64]{3,2,1,0:T(8,128)} %fusion.383), custom_call_target="InvertDiagBlocksLowerTriangular" | custom-call | tf_op jit(solution)/shard_map/while/body/eval_jaxpr/jit(_solve_triangular)/vmap()/triangular_solve | solution.py:67
  146.6 10.6 %custom-call.50 = f32[2,1,64,64]{2,3,1,0:T(8,128)S(1)} custom-call(f32[2,1,64,64]{3,2,1,0:T(8,128)} %fusion.383), custom_call_target="InvertDiagBlocksLowerTriangular" | custom-call | tf_op jit(solution)/shard_map/while/body/eval_jaxpr/jit(_solve_triangular)/vmap()/triangular_solve | solution.py:67
  162.5 3.3 collective-permute-start.18
  167.2 1.9 collective-permute-start.22
  169.2 3.9 collective-permute-start.8
  173.1 2.6 collective-permute-start.12
  177.3 3.9 collective-permute-start.19
  181.7 2.3 collective-permute-start.23
  184.3 4.5 collective-permute-start.9
  189.0 5.6 collective-permute-start.13
  194.9 3.6 collective-permute-start.20
  198.8 6.4 %collective-permute-start.24 = (f32[2,128,128]{2,1,0:T(8,128)S(1)}, f32[2,128,128]{2,1,0:T(8,128)S(1)}, u32[]{:S(2)}, u32[]{:S(2)}) collective-permute-start(f32[2,128,128]{2,1,0:T(8,128)S(1)} %convolution_add_fusion.15), channel_id=1, source_target_pairs={{32,0},{40,8},{48,16},{56,24},{64,32},{72,40},{80,48},{88,56},{96,... | collective-permute-start | bytes 393224 | tf_op jit(solution)/shard_map/ppermute | solution.py:17
  205.5 4.3 collective-permute-start.10
  210.0 19.7 %collective-permute-start.14 = (f32[2,128,128]{2,1,0:T(8,128)S(1)}, f32[2,128,128]{2,1,0:T(8,128)S(1)}, u32[]{:S(2)}, u32[]{:S(2)}) collective-permute-start(f32[2,128,128]{2,1,0:T(8,128)S(1)} %convolution_add_fusion.20), channel_id=1, source_target_pairs={{0,32},{8,40},{16,48},{24,56},{32,64},{40,72},{48,80},{56,88},{64,... | collective-permute-start | bytes 393224 | tf_op jit(solution)/shard_map/ppermute | solution.py:17
  230.0 4.5 collective-permute-start.21
  234.8 1.9 collective-permute-start.25
  237.1 3.9 collective-permute-start.11
  241.3 1.9 collective-permute-start.15
  245.0 3.2 collective-permute-done.15
  248.4 2.9 collective-permute-start.16
  251.9 1.9 collective-permute-done.16
  254.1 1.9 collective-permute-start.17
  257.0 3.9 collective-permute-start.27
  264.6 106.0 %while.103 = (s32[]{:T(128)}, f32[2,128,128]{2,1,0:T(8,128)S(1)}, bf16[4,2,64,128]{3,2,1,0:T(8,128)(2,1)}, f32[4,2,64,64]{3,2,1,0:T(8,128)}, f32[4,2,64]{2,1,0:T...) while((s32[]{:T(128)}, f32[2,128,128]{2,1,0:T(8,128)S(1)}, ...), condition=%wide.region_11.12_spmd.clone.clone, body=%wide.region_9.11_spmd.clone.clone.sunk | while | flops 126304576 | bytes 3354481 | solution.py:94
  271.2 10.6 %custom-call.51 = f32[2,1,64,64]{2,3,1,0:T(8,128)S(1)} custom-call(f32[2,1,64,64]{3,2,1,0:T(8,128)} %add_bitcast_fusion.4), custom_call_target="InvertDiagBlocksLowerTriangular" | custom-call | tf_op jit(solution)/shard_map/jvp()/while/body/eval_jaxpr/jit(_solve_triangular)/vmap()/triangular_solve | solution.py:67
  297.6 10.6 %custom-call.51 = f32[2,1,64,64]{2,3,1,0:T(8,128)S(1)} custom-call(f32[2,1,64,64]{3,2,1,0:T(8,128)} %add_bitcast_fusion.4), custom_call_target="InvertDiagBlocksLowerTriangular" | custom-call | tf_op jit(solution)/shard_map/jvp()/while/body/eval_jaxpr/jit(_solve_triangular)/vmap()/triangular_solve | solution.py:67
  324.1 10.6 %custom-call.51 = f32[2,1,64,64]{2,3,1,0:T(8,128)S(1)} custom-call(f32[2,1,64,64]{3,2,1,0:T(8,128)} %add_bitcast_fusion.4), custom_call_target="InvertDiagBlocksLowerTriangular" | custom-call | tf_op jit(solution)/shard_map/jvp()/while/body/eval_jaxpr/jit(_solve_triangular)/vmap()/triangular_solve | solution.py:67
  350.6 10.6 %custom-call.51 = f32[2,1,64,64]{2,3,1,0:T(8,128)S(1)} custom-call(f32[2,1,64,64]{3,2,1,0:T(8,128)} %add_bitcast_fusion.4), custom_call_target="InvertDiagBlocksLowerTriangular" | custom-call | tf_op jit(solution)/shard_map/jvp()/while/body/eval_jaxpr/jit(_solve_triangular)/vmap()/triangular_solve | solution.py:67
  372.8 138.2 %while.104 = (s32[]{:T(128)}, f32[2,128,128]{2,1,0:T(8,128)S(1)}, f32[4,2,64,128]{3,2,1,0:T(8,128)}, f32[4,2,64,128]{3,2,1,0:T(8,128)}, bf16[4,2,64,128]{3,2,0,1...) while((s32[]{:T(128)}, f32[2,128,128]{2,1,0:T(8,128)S(1)}, ...), condition=%wide.region_23.24_spmd.clone.clone, body=%wide.region_12.23_spmd.clone.clone.sunk | while | flops 258745024 | bytes 5340221 | solution.py:94
  377.2 9.8 %custom-call.52 = f32[2,1,64,64]{2,3,1,0:T(8,128)S(1)} custom-call(f32[2,1,64,64]{3,2,1,0:T(8,128)S(1)} %add_bitcast_fusion.5), custom_call_target="InvertDiagBlocksLowerTriangular" | custom-call | tf_op jit(solution)/shard_map/transpose(jvp())/while/body/eval_jaxpr/jit(_solve_triangular)/vmap()/triangular_solve | solution.py:67
  411.7 9.8 %custom-call.52 = f32[2,1,64,64]{2,3,1,0:T(8,128)S(1)} custom-call(f32[2,1,64,64]{3,2,1,0:T(8,128)S(1)} %add_bitcast_fusion.5), custom_call_target="InvertDiagBlocksLowerTriangular" | custom-call | tf_op jit(solution)/shard_map/transpose(jvp())/while/body/eval_jaxpr/jit(_solve_triangular)/vmap()/triangular_solve | solution.py:67
  446.3 9.8 %custom-call.52 = f32[2,1,64,64]{2,3,1,0:T(8,128)S(1)} custom-call(f32[2,1,64,64]{3,2,1,0:T(8,128)S(1)} %add_bitcast_fusion.5), custom_call_target="InvertDiagBlocksLowerTriangular" | custom-call | tf_op jit(solution)/shard_map/transpose(jvp())/while/body/eval_jaxpr/jit(_solve_triangular)/vmap()/triangular_solve | solution.py:67
  480.8 9.8 %custom-call.52 = f32[2,1,64,64]{2,3,1,0:T(8,128)S(1)} custom-call(f32[2,1,64,64]{3,2,1,0:T(8,128)S(1)} %add_bitcast_fusion.5), custom_call_target="InvertDiagBlocksLowerTriangular" | custom-call | tf_op jit(solution)/shard_map/transpose(jvp())/while/body/eval_jaxpr/jit(_solve_triangular)/vmap()/triangular_solve | solution.py:67
  515.0 12.6 %psum.15 = f32[256]{0:T(256)S(1)} all-reduce(f32[256]{0:T(256)S(1)} %get-tuple-element.1871), channel_id=1, replica_groups=mesh['seq'=32,'head'=8] {'head'}, use_global_device_ids=true, to_apply=%region_25.26 | all-reduce | flops 256 | bytes 2048 | tf_op jit(solution)/shard_map/psum | solution.py:216
  528.4 3.3 fusion.240
  534.6 2.7 fusion.239
  537.3 2.3 fusion.198
  542.7 3.1 collective-permute-done.36
  546.0 4.3 collective-permute-done.37
  552.2 5.6 collective-permute-done.38
  557.8 2.0 collective-permute-start.39
  559.8 1.9 collective-permute-start.32
  561.8 1.9 collective-permute-start.33
  563.7 5.5 collective-permute-start.34
  569.2 4.3 collective-permute-start.35
  573.5 4.0 collective-permute-start.40
  580.5 2.5 collective-permute-start.28
  583.5 2.7 collective-permute-start.29
  586.2 7.2 %collective-permute-start.30 = (bf16[256,2,128]{2,0,1:T(8,128)(2,1)S(1)}, bf16[256,2,128]{2,0,1:T(8,128)(2,1)S(1)}, u32[]{:S(2)}, u32[]{:S(2)}) collective-permute-start(bf16[256,2,128]{2,0,1:T(8,128)(2,1)S(1)} %get-tuple-element.2064), channel_id=1, source_target_pairs={{24,0},{32,8},{40,16},{48,24},{56,32},{64,40},{72,48},{80,56},{88,... | collective-permute-start | bytes 393224 | tf_op jit(solution)/shard_map/ppermute | solution.py:17
  597.2 12.7 %collective-permute-done.30 = bf16[256,2,128]{2,0,1:T(8,128)(2,1)S(1)} collective-permute-done((bf16[256,2,128]{2,0,1:T(8,128)(2,1)S(1)}, bf16[256,2,128]{2,0,1:T(8,128)(2,1)S(1)}, u32[]{:S(2)}, u32[]{:S(2)}) %collective-permute-start.30) | collective-permute-done | bytes 131104 | tf_op jit(solution)/shard_map/ppermute | solution.py:17
  (584 shorter events, 263.4 us)
Async XLA Ops:
  0.6 44.8 %copy-start = (bf16[256,2,128]{2,1,0:T(2,128)(2,1)S(1)}, bf16[256,2,128]{2,1,0:T(2,128)(2,1)}, u32[]{:S(2)}) copy-start(bf16[256,2,128]{2,1,0:T(2,128)(2,1)} %param.23) | copy-start | bytes 393220
  0.7 28.9 %copy-start.17 = (bf16[256,2,128]{2,1,0:T(2,128)(2,1)S(1)}, bf16[256,2,128]{2,1,0:T(2,128)(2,1)}, u32[]{:S(2)}) copy-start(bf16[256,2,128]{2,1,0:T(2,128)(2,1)} %param.31) | copy-start | bytes 393220
  0.7 32.3 %copy-start.45 = (f32[256,2]{0,1:T(2,128)S(1)}, f32[256,2]{0,1:T(2,128)}, u32[]{:S(2)}) copy-start(f32[256,2]{0,1:T(2,128)} %param.30) | copy-start | bytes 6148
  0.7 33.0 %copy-start.46 = (f32[256,2]{0,1:T(2,128)S(1)}, f32[256,2]{0,1:T(2,128)}, u32[]{:S(2)}) copy-start(f32[256,2]{0,1:T(2,128)} %param.29) | copy-start | bytes 6148
  1.7 32.7 %collective-permute-start.4 = (bf16[256,2,128]{2,0,1:T(8,128)(2,1)S(1)}, bf16[256,2,128]{2,0,1:T(8,128)(2,1)S(1)}, u32[]{:S(2)}, u32[]{:S(2)}) collective-permute-start(bf16[256,2,128]{2,0,1:T(8,128)(2,1)S(1)} %copy.256), channel_id=1, source_target_pairs={{0,32},{8,40},{16,48},{24,56},{32,64},{40,72},{48,80},{56,88},{64,... | collective-permute-start | bytes 393224 | tf_op jit(solution)/shard_map/ppermute | solution.py:17
  4.2 36.2 %collective-permute-start.5 = (bf16[256,2,128]{2,0,1:T(8,128)(2,1)S(1)}, bf16[256,2,128]{2,0,1:T(8,128)(2,1)S(1)}, u32[]{:S(2)}, u32[]{:S(2)}) collective-permute-start(bf16[256,2,128]{2,0,1:T(8,128)(2,1)S(1)} %copy.256), channel_id=1, source_target_pairs={{0,24},{8,32},{16,40},{24,48},{32,56},{40,64},{48,72},{56,80},{64,... | collective-permute-start | bytes 393224 | tf_op jit(solution)/shard_map/ppermute | solution.py:17
  11.9 30.9 %collective-permute-start.6 = (bf16[256,2,128]{2,0,1:T(8,128)(2,1)S(1)}, bf16[256,2,128]{2,0,1:T(8,128)(2,1)S(1)}, u32[]{:S(2)}, u32[]{:S(2)}) collective-permute-start(bf16[256,2,128]{2,0,1:T(8,128)(2,1)S(1)} %copy.256), channel_id=1, source_target_pairs={{0,16},{8,24},{16,32},{24,40},{32,48},{40,56},{48,64},{56,72},{64,... | collective-permute-start | bytes 393224 | tf_op jit(solution)/shard_map/ppermute | solution.py:17
  15.3 30.0 %collective-permute-start.7 = (bf16[256,2,128]{2,0,1:T(8,128)(2,1)S(1)}, bf16[256,2,128]{2,0,1:T(8,128)(2,1)S(1)}, u32[]{:S(2)}, u32[]{:S(2)}) collective-permute-start(bf16[256,2,128]{2,0,1:T(8,128)(2,1)S(1)} %copy.256), channel_id=1, source_target_pairs={{0,8},{8,16},{16,24},{24,32},{32,40},{40,48},{48,56},{56,64},{64,7... | collective-permute-start | bytes 393224 | tf_op jit(solution)/shard_map/ppermute | solution.py:17
  19.3 28.8 %collective-permute-start = (bf16[256,2,128]{0,2,1:T(8,128)(2,1)S(1)}, bf16[256,2,128]{0,2,1:T(8,128)(2,1)}, u32[]{:S(2)}, u32[]{:S(2)}) collective-permute-start(bf16[256,2,128]{0,2,1:T(8,128)(2,1)S(1)} %copy.251), channel_id=1, source_target_pairs={{0,32},{8,40},{16,48},{24,56},{32,64},{40,72},{48,80},{56,88},{64,... | collective-permute-start | bytes 393224 | tf_op jit(solution)/shard_map/ppermute | solution.py:17
  26.7 18.7 %copy-start.15 = (bf16[256,2,128]{2,1,0:T(2,128)(2,1)S(1)}, bf16[256,2,128]{2,1,0:T(2,128)(2,1)}, u32[]{:S(2)}) copy-start(bf16[256,2,128]{2,1,0:T(2,128)(2,1)} %param.24) | copy-start | bytes 393220
  34.4 14.7 %collective-permute-start.1 = (bf16[256,2,128]{0,2,1:T(8,128)(2,1)S(1)}, bf16[256,2,128]{0,2,1:T(8,128)(2,1)S(1)}, u32[]{:S(2)}, u32[]{:S(2)}) collective-permute-start(bf16[256,2,128]{0,2,1:T(8,128)(2,1)S(1)} %copy.251), channel_id=1, source_target_pairs={{0,24},{8,32},{16,40},{24,48},{32,56},{40,64},{48,72},{56,80},{64,... | collective-permute-start | bytes 393224 | tf_op jit(solution)/shard_map/ppermute | solution.py:17
  40.4 15.5 %collective-permute-start.2 = (bf16[256,2,128]{0,2,1:T(8,128)(2,1)S(1)}, bf16[256,2,128]{0,2,1:T(8,128)(2,1)S(1)}, u32[]{:S(2)}, u32[]{:S(2)}) collective-permute-start(bf16[256,2,128]{0,2,1:T(8,128)(2,1)S(1)} %copy.251), channel_id=1, source_target_pairs={{0,16},{8,24},{16,32},{24,40},{32,48},{40,56},{48,64},{56,72},{64,... | collective-permute-start | bytes 393224 | tf_op jit(solution)/shard_map/ppermute | solution.py:17
  42.8 15.3 %collective-permute-start.3 = (bf16[256,2,128]{0,2,1:T(8,128)(2,1)S(1)}, bf16[256,2,128]{0,2,1:T(8,128)(2,1)S(1)}, u32[]{:S(2)}, u32[]{:S(2)}) collective-permute-start(bf16[256,2,128]{0,2,1:T(8,128)(2,1)S(1)} %copy.251), channel_id=1, source_target_pairs={{0,8},{8,16},{16,24},{24,32},{32,40},{40,48},{48,56},{56,64},{64,7... | collective-permute-start | bytes 393224 | tf_op jit(solution)/shard_map/ppermute | solution.py:17
  48.0 26.0 %copy-start.39 = (f32[2,128]{1,0:T(2,128)S(1)}, f32[2,128]{1,0:T(2,128)}, u32[]{:S(2)}) copy-start(f32[2,128]{1,0:T(2,128)} %param.26) | copy-start | bytes 3076
  59.0 19.4 %copy-start.2 = (f32[2,128,256]{2,1,0:T(8,128)}, f32[2,128,256]{2,1,0:T(8,128)S(1)}, u32[]{:S(2)}) copy-start(f32[2,128,256]{2,1,0:T(8,128)S(1)} %get-tuple-element.2072) | copy-start | bytes 786436
  162.5 14.4 %collective-permute-start.18 = (f32[2,128,128]{1,2,0:T(8,128)S(1)}, f32[2,128,128]{1,2,0:T(8,128)S(1)}, u32[]{:S(2)}, u32[]{:S(2)}) collective-permute-start(f32[2,128,128]{1,2,0:T(8,128)S(1)} %get-tuple-element.2066), channel_id=1, source_target_pairs={{8,0},{16,8},{24,16},{32,24},{40,32},{48,40},{56,48},{64,56},{72,6... | collective-permute-start | bytes 393224 | tf_op jit(solution)/shard_map/ppermute | solution.py:17
  167.2 14.0 %collective-permute-start.22 = (f32[2,128,128]{2,1,0:T(8,128)S(1)}, f32[2,128,128]{2,1,0:T(8,128)S(1)}, u32[]{:S(2)}, u32[]{:S(2)}) collective-permute-start(f32[2,128,128]{2,1,0:T(8,128)S(1)} %fusion.203), channel_id=1, source_target_pairs={{8,0},{16,8},{24,16},{32,24},{40,32},{48,40},{56,48},{64,56},{72,6... | collective-permute-start | bytes 393224 | tf_op jit(solution)/shard_map/ppermute | solution.py:17
  169.2 14.8 %collective-permute-start.8 = (f32[2,128,128]{2,1,0:T(8,128)S(1)}, f32[2,128,128]{2,1,0:T(8,128)S(1)}, u32[]{:S(2)}, u32[]{:S(2)}) collective-permute-start(f32[2,128,128]{2,1,0:T(8,128)S(1)} %get-tuple-element.2068), channel_id=1, source_target_pairs={{0,8},{8,16},{16,24},{24,32},{32,40},{40,48},{48,56},{56,64},{64,7... | collective-permute-start | bytes 393224 | tf_op jit(solution)/shard_map/ppermute | solution.py:17
  173.1 15.6 %collective-permute-start.12 = (f32[2,128,128]{2,1,0:T(8,128)S(1)}, f32[2,128,128]{2,1,0:T(8,128)S(1)}, u32[]{:S(2)}, u32[]{:S(2)}) collective-permute-start(f32[2,128,128]{2,1,0:T(8,128)S(1)} %get-tuple-element.2067), channel_id=1, source_target_pairs={{0,8},{8,16},{16,24},{24,32},{32,40},{40,48},{48,56},{56,64},{64,7... | collective-permute-start | bytes 393224 | tf_op jit(solution)/shard_map/ppermute | solution.py:17
  177.3 17.3 %collective-permute-start.19 = (f32[2,128,128]{2,1,0:T(8,128)S(1)}, f32[2,128,128]{2,1,0:T(8,128)S(1)}, u32[]{:S(2)}, u32[]{:S(2)}) collective-permute-start(f32[2,128,128]{2,1,0:T(8,128)S(1)} %fusion.227), channel_id=1, source_target_pairs={{16,0},{24,8},{32,16},{40,24},{48,32},{56,40},{64,48},{72,56},{80,... | collective-permute-start | bytes 393224 | tf_op jit(solution)/shard_map/ppermute | solution.py:17
  181.7 16.8 %collective-permute-start.23 = (f32[2,128,128]{2,1,0:T(8,128)S(1)}, f32[2,128,128]{2,1,0:T(8,128)S(1)}, u32[]{:S(2)}, u32[]{:S(2)}) collective-permute-start(f32[2,128,128]{2,1,0:T(8,128)S(1)} %convolution_add_fusion.16), channel_id=1, source_target_pairs={{16,0},{24,8},{32,16},{40,24},{48,32},{56,40},{64,48},{72,56},{80,... | collective-permute-start | bytes 393224 | tf_op jit(solution)/shard_map/ppermute | solution.py:17
  184.3 20.9 %collective-permute-start.9 = (f32[2,128,128]{2,1,0:T(8,128)S(1)}, f32[2,128,128]{2,1,0:T(8,128)S(1)}, u32[]{:S(2)}, u32[]{:S(2)}) collective-permute-start(f32[2,128,128]{2,1,0:T(8,128)S(1)} %fusion.230), channel_id=1, source_target_pairs={{0,16},{8,24},{16,32},{24,40},{32,48},{40,56},{48,64},{56,72},{64,... | collective-permute-start | bytes 393224 | tf_op jit(solution)/shard_map/ppermute | solution.py:17
  189.0 20.7 %collective-permute-start.13 = (f32[2,128,128]{2,1,0:T(8,128)S(1)}, f32[2,128,128]{2,1,0:T(8,128)S(1)}, u32[]{:S(2)}, u32[]{:S(2)}) collective-permute-start(f32[2,128,128]{2,1,0:T(8,128)S(1)} %convolution_add_fusion.21), channel_id=1, source_target_pairs={{0,16},{8,24},{16,32},{24,40},{32,48},{40,56},{48,64},{56,72},{64,... | collective-permute-start | bytes 393224 | tf_op jit(solution)/shard_map/ppermute | solution.py:17
  194.9 34.9 %collective-permute-start.20 = (f32[2,128,128]{2,1,0:T(8,128)S(1)}, f32[2,128,128]{2,1,0:T(8,128)S(1)}, u32[]{:S(2)}, u32[]{:S(2)}) collective-permute-start(f32[2,128,128]{2,1,0:T(8,128)S(1)} %fusion.244), channel_id=1, source_target_pairs={{32,0},{40,8},{48,16},{56,24},{64,32},{72,40},{80,48},{88,56},{96,... | collective-permute-start | bytes 393224 | tf_op jit(solution)/shard_map/ppermute | solution.py:17
  198.8 35.7 %collective-permute-start.24 = (f32[2,128,128]{2,1,0:T(8,128)S(1)}, f32[2,128,128]{2,1,0:T(8,128)S(1)}, u32[]{:S(2)}, u32[]{:S(2)}) collective-permute-start(f32[2,128,128]{2,1,0:T(8,128)S(1)} %convolution_add_fusion.15), channel_id=1, source_target_pairs={{32,0},{40,8},{48,16},{56,24},{64,32},{72,40},{80,48},{88,56},{96,... | collective-permute-start | bytes 393224 | tf_op jit(solution)/shard_map/ppermute | solution.py:17
  205.5 31.3 %collective-permute-start.10 = (f32[2,128,128]{2,1,0:T(8,128)S(1)}, f32[2,128,128]{2,1,0:T(8,128)S(1)}, u32[]{:S(2)}, u32[]{:S(2)}) collective-permute-start(f32[2,128,128]{2,1,0:T(8,128)S(1)} %fusion.241), channel_id=1, source_target_pairs={{0,32},{8,40},{16,48},{24,56},{32,64},{40,72},{48,80},{56,88},{64,... | collective-permute-start | bytes 393224 | tf_op jit(solution)/shard_map/ppermute | solution.py:17
  210.0 30.9 %collective-permute-start.14 = (f32[2,128,128]{2,1,0:T(8,128)S(1)}, f32[2,128,128]{2,1,0:T(8,128)S(1)}, u32[]{:S(2)}, u32[]{:S(2)}) collective-permute-start(f32[2,128,128]{2,1,0:T(8,128)S(1)} %convolution_add_fusion.20), channel_id=1, source_target_pairs={{0,32},{8,40},{16,48},{24,56},{32,64},{40,72},{48,80},{56,88},{64,... | collective-permute-start | bytes 393224 | tf_op jit(solution)/shard_map/ppermute | solution.py:17
  230.0 21.3 %collective-permute-start.21 = (f32[2,128,128]{2,1,0:T(8,128)S(1)}, f32[2,128,128]{2,1,0:T(8,128)S(1)}, u32[]{:S(2)}, u32[]{:S(2)}) collective-permute-start(f32[2,128,128]{2,1,0:T(8,128)S(1)} %fusion.245), channel_id=1, source_target_pairs={{64,0},{72,8},{80,16},{88,24},{96,32},{104,40},{112,48},{120,56},{... | collective-permute-start | bytes 393224 | tf_op jit(solution)/shard_map/ppermute | solution.py:17
  234.8 29.8 %copy-start.42 = (f32[4,2,64,1]{2,1,3,0:T(2,128)S(1)}, f32[4,2,64,1]{2,1,3,0:T(2,128)}, u32[]{:S(2)}) copy-start(f32[4,2,64,1]{2,1,3,0:T(2,128)} %custom-call.34) | copy-start | bytes 6148
  234.8 8.4 %collective-permute-start.25 = (f32[2,128,128]{2,1,0:T(8,128)S(1)}, f32[2,128,128]{2,1,0:T(8,128)S(1)}, u32[]{:S(2)}, u32[]{:S(2)}) collective-permute-start(f32[2,128,128]{2,1,0:T(8,128)S(1)} %convolution_add_fusion.14), channel_id=1, source_target_pairs={{64,0},{72,8},{80,16},{88,24},{96,32},{104,40},{112,48},{120,56},{... | collective-permute-start | bytes 393224 | tf_op jit(solution)/shard_map/ppermute | solution.py:17
  237.1 14.6 %collective-permute-start.11 = (f32[2,128,128]{2,1,0:T(8,128)S(1)}, f32[2,128,128]{2,1,0:T(8,128)S(1)}, u32[]{:S(2)}, u32[]{:S(2)}) collective-permute-start(f32[2,128,128]{2,1,0:T(8,128)S(1)} %fusion.242), channel_id=1, source_target_pairs={{0,64},{8,72},{16,80},{24,88},{32,96},{40,104},{48,112},{56,120},{... | collective-permute-start | bytes 393224 | tf_op jit(solution)/shard_map/ppermute | solution.py:17
  241.3 6.9 %collective-permute-start.15 = (f32[2,128,128]{2,1,0:T(8,128)S(1)}, f32[2,128,128]{2,1,0:T(8,128)S(1)}, u32[]{:S(2)}, u32[]{:S(2)}) collective-permute-start(f32[2,128,128]{2,1,0:T(8,128)S(1)} %convolution_add_fusion.19), channel_id=1, source_target_pairs={{0,64},{8,72},{16,80},{24,88},{32,96},{40,104},{48,112},{56,120},{... | collective-permute-start | bytes 393224 | tf_op jit(solution)/shard_map/ppermute | solution.py:17
  243.5 12.5 %collective-permute-start.26 = (f32[2,128,128]{2,1,0:T(8,128)S(1)}, f32[2,128,128]{2,1,0:T(8,128)S(1)}, u32[]{:S(2)}, u32[]{:S(2)}) collective-permute-start(f32[2,128,128]{2,1,0:T(8,128)S(1)} %convolution_add_fusion.13), channel_id=1, source_target_pairs={{128,0},{136,8},{144,16},{152,24},{160,32},{168,40},{176,48},{184,... | collective-permute-start | bytes 393224 | tf_op jit(solution)/shard_map/ppermute | solution.py:17
  248.4 5.4 collective-permute-start.16
  254.1 6.9 %collective-permute-start.17 = (f32[2,128,128]{2,1,0:T(8,128)S(1)}, f32[2,128,128]{2,1,0:T(8,128)S(1)}, u32[]{:S(2)}, u32[]{:S(2)}) collective-permute-start(f32[2,128,128]{2,1,0:T(8,128)S(1)} %convolution_add_fusion.17), channel_id=1, source_target_pairs={{0,8},{8,16},{16,24},{24,32},{32,40},{40,48},{48,56},{56,64},{64,7... | collective-permute-start | bytes 393224 | tf_op jit(solution)/shard_map/ppermute | solution.py:17
  257.0 113.7 %collective-permute-start.27 = (f32[2,128,128]{2,1,0:T(8,128)}, f32[2,128,128]{2,1,0:T(8,128)S(1)}, u32[]{:S(2)}, u32[]{:S(2)}) collective-permute-start(f32[2,128,128]{2,1,0:T(8,128)} %convolution_add_fusion.12), channel_id=1, source_target_pairs={{8,0},{16,8},{24,16},{32,24},{40,32},{48,40},{56,48},{64,56},{72,6... | collective-permute-start | bytes 393224 | tf_op jit(solution)/shard_map/ppermute | solution.py:17
  372.8 140.5 %copy-start.28 = (f32[256]{0:T(256)S(1)}, f32[256]{0:T(256)}, u32[]{:S(2)}) copy-start(f32[256]{0:T(256)} %copy-done.27) | copy-start | bytes 3076
  372.8 20.9 %copy-start.29 = (f32[4,2,64]{2,1,0:T(2,128)}, f32[4,2,64]{2,1,0:T(2,128)S(1)}, u32[]{:S(2)}) copy-start(f32[4,2,64]{2,1,0:T(2,128)S(1)} %get-tuple-element.2808) | copy-start | bytes 6148 | tf_op jit(solution)/shard_map/transpose(jvp())/while
  407.4 20.9 %copy-start.29 = (f32[4,2,64]{2,1,0:T(2,128)}, f32[4,2,64]{2,1,0:T(2,128)S(1)}, u32[]{:S(2)}) copy-start(f32[4,2,64]{2,1,0:T(2,128)S(1)} %get-tuple-element.2808) | copy-start | bytes 6148 | tf_op jit(solution)/shard_map/transpose(jvp())/while
  441.9 20.9 %copy-start.29 = (f32[4,2,64]{2,1,0:T(2,128)}, f32[4,2,64]{2,1,0:T(2,128)S(1)}, u32[]{:S(2)}) copy-start(f32[4,2,64]{2,1,0:T(2,128)S(1)} %get-tuple-element.2808) | copy-start | bytes 6148 | tf_op jit(solution)/shard_map/transpose(jvp())/while
  476.5 20.9 %copy-start.29 = (f32[4,2,64]{2,1,0:T(2,128)}, f32[4,2,64]{2,1,0:T(2,128)S(1)}, u32[]{:S(2)}) copy-start(f32[4,2,64]{2,1,0:T(2,128)S(1)} %get-tuple-element.2808) | copy-start | bytes 6148 | tf_op jit(solution)/shard_map/transpose(jvp())/while
  498.3 12.7 %copy-start.30 = (f32[4,2,64]{2,1,0:T(2,128)S(1)}, f32[4,2,64]{2,1,0:T(2,128)}, u32[]{:S(2)}) copy-start(f32[4,2,64]{2,1,0:T(2,128)} %copy-done.29) | copy-start | bytes 6148 | tf_op jit(solution)/shard_map/transpose(jvp())/while
  512.2 19.5 %copy-start.3 = (f32[2,128,256]{2,1,0:T(8,128)S(1)}, f32[2,128,256]{2,1,0:T(8,128)}, u32[]{:S(2)}) copy-start(f32[2,128,256]{2,1,0:T(8,128)} %copy-done.2) | copy-start | bytes 786436
  512.2 19.5 %copy-start.22 = (f32[2,256]{1,0:T(2,128)S(1)}, f32[2,256]{1,0:T(2,128)}, u32[]{:S(2)}) copy-start(f32[2,256]{1,0:T(2,128)} %copy-done.21) | copy-start | bytes 6148
  512.2 19.5 %copy-start.40 = (f32[2,128]{1,0:T(2,128)S(1)}, f32[2,128]{1,0:T(2,128)}, u32[]{:S(2)}) copy-start(f32[2,128]{1,0:T(2,128)} %param.26) | copy-start | bytes 3076
  539.7 20.1 %copy-start.6 = (bf16[1280,2,128]{0,2,1:T(8,128)(2,1)S(1)}, bf16[1280,2,128]{0,2,1:T(8,128)(2,1)}, u32[]{:S(2)}) copy-start(bf16[1280,2,128]{0,2,1:T(8,128)(2,1)} %get-tuple-element.2077) | copy-start | bytes 1966084
  539.7 37.8 %copy-start.18 = (bf16[1280,2,128]{2,0,1:T(8,128)(2,1)S(1)}, bf16[1280,2,128]{2,0,1:T(8,128)(2,1)}, u32[]{:S(2)}) copy-start(bf16[1280,2,128]{2,0,1:T(8,128)(2,1)} %get-tuple-element.2075) | copy-start | bytes 1966084
  540.3 37.3 %copy-start.20 = (bf16[256,2,128]{2,0,1:T(8,128)(2,1)S(1)}, bf16[256,2,128]{2,0,1:T(8,128)(2,1)}, u32[]{:S(2)}) copy-start(bf16[256,2,128]{2,0,1:T(8,128)(2,1)} %fusion.198) | copy-start | bytes 393220
  540.5 37.8 %copy-start.36 = (f32[4,2,64]{2,1,0:T(2,128)S(1)}, f32[4,2,64]{2,1,0:T(2,128)}, u32[]{:S(2)}) copy-start(f32[4,2,64]{2,1,0:T(2,128)} %copy-done.35) | copy-start | bytes 6148
  540.6 38.5 %copy-start.38 = (f32[4,2,64]{2,1,0:T(2,128)S(1)}, f32[4,2,64]{2,1,0:T(2,128)}, u32[]{:S(2)}) copy-start(f32[4,2,64]{2,1,0:T(2,128)} %copy-done.37) | copy-start | bytes 6148
  540.6 39.1 %copy-start.16 = (bf16[4,2,64,128]{3,2,1,0:T(8,128)(2,1)S(1)}, bf16[4,2,64,128]{3,2,1,0:T(8,128)(2,1)}, u32[]{:S(2)}) copy-start(bf16[4,2,64,128]{3,2,1,0:T(8,128)(2,1)} %get-tuple-element.1225) | copy-start | bytes 393220
  542.2 3.7 collective-permute-start.36
  545.8 4.5 collective-permute-start.37
  550.3 7.5 %collective-permute-start.38 = (f32[2,128]{1,0:T(2,128)S(1)}, f32[2,128]{1,0:T(2,128)S(1)}, u32[]{:S(2)}, u32[]{:S(2)}) collective-permute-start(f32[2,128]{1,0:T(2,128)S(1)} %add.295), channel_id=1, source_target_pairs={{0,32},{8,40},{16,48},{24,56},{32,0},{40,8},{48,16},{56,24},{64,96... | collective-permute-start | bytes 3080 | tf_op jit(solution)/shard_map/ppermute | solution.py:42
  557.8 15.7 %collective-permute-start.39 = (f32[2,128]{1,0:T(2,128)S(1)}, f32[2,128]{1,0:T(2,128)S(1)}, u32[]{:S(2)}, u32[]{:S(2)}) collective-permute-start(f32[2,128]{1,0:T(2,128)S(1)} %add.296), channel_id=1, source_target_pairs={{0,64},{8,72},{16,80},{24,88},{32,96},{40,104},{48,112},{56,120},{... | collective-permute-start | bytes 3080 | tf_op jit(solution)/shard_map/ppermute | solution.py:42
  559.8 23.7 %collective-permute-start.32 = (bf16[256,2,128]{0,2,1:T(8,128)(2,1)S(1)}, bf16[256,2,128]{0,2,1:T(8,128)(2,1)S(1)}, u32[]{:S(2)}, u32[]{:S(2)}) collective-permute-start(bf16[256,2,128]{0,2,1:T(8,128)(2,1)S(1)} %get-tuple-element.2058), channel_id=1, source_target_pairs={{8,0},{16,8},{24,16},{32,24},{40,32},{48,40},{56,48},{64,56},{72,6... | collective-permute-start | bytes 393224 | tf_op jit(solution)/shard_map/ppermute | solution.py:17
  561.8 24.4 %collective-permute-start.33 = (bf16[256,2,128]{0,2,1:T(8,128)(2,1)S(1)}, bf16[256,2,128]{0,2,1:T(8,128)(2,1)S(1)}, u32[]{:S(2)}, u32[]{:S(2)}) collective-permute-start(bf16[256,2,128]{0,2,1:T(8,128)(2,1)S(1)} %get-tuple-element.2061), channel_id=1, source_target_pairs={{16,0},{24,8},{32,16},{40,24},{48,32},{56,40},{64,48},{72,56},{80,... | collective-permute-start | bytes 393224 | tf_op jit(solution)/shard_map/ppermute | solution.py:17
  563.7 29.7 %collective-permute-start.34 = (bf16[256,2,128]{0,2,1:T(8,128)(2,1)S(1)}, bf16[256,2,128]{0,2,1:T(8,128)(2,1)S(1)}, u32[]{:S(2)}, u32[]{:S(2)}) collective-permute-start(bf16[256,2,128]{0,2,1:T(8,128)(2,1)S(1)} %get-tuple-element.2060), channel_id=1, source_target_pairs={{24,0},{32,8},{40,16},{48,24},{56,32},{64,40},{72,48},{80,56},{88,... | collective-permute-start | bytes 393224 | tf_op jit(solution)/shard_map/ppermute | solution.py:17
  569.2 26.2 %collective-permute-start.35 = (bf16[256,2,128]{0,2,1:T(8,128)(2,1)S(1)}, bf16[256,2,128]{0,2,1:T(8,128)(2,1)S(1)}, u32[]{:S(2)}, u32[]{:S(2)}) collective-permute-start(bf16[256,2,128]{0,2,1:T(8,128)(2,1)S(1)} %get-tuple-element.2059), channel_id=1, source_target_pairs={{32,0},{40,8},{48,16},{56,24},{64,32},{72,40},{80,48},{88,56},{96,... | collective-permute-start | bytes 393224 | tf_op jit(solution)/shard_map/ppermute | solution.py:17
  573.5 7.0 %collective-permute-start.40 = (f32[2,128]{1,0:T(2,128)S(1)}, f32[2,128]{1,0:T(2,128)S(1)}, u32[]{:S(2)}, u32[]{:S(2)}) collective-permute-start(f32[2,128]{1,0:T(2,128)S(1)} %add.297), channel_id=1, source_target_pairs={{0,128},{8,136},{16,144},{24,152},{32,160},{40,168},{48,176},{56,1... | collective-permute-start | bytes 3080 | tf_op jit(solution)/shard_map/ppermute | solution.py:42
  580.5 16.7 %collective-permute-start.28 = (bf16[256,2,128]{2,0,1:T(8,128)(2,1)S(1)}, bf16[256,2,128]{2,0,1:T(8,128)(2,1)S(1)}, u32[]{:S(2)}, u32[]{:S(2)}) collective-permute-start(bf16[256,2,128]{2,0,1:T(8,128)(2,1)S(1)} %get-tuple-element.2062), channel_id=1, source_target_pairs={{8,0},{16,8},{24,16},{32,24},{40,32},{48,40},{56,48},{64,56},{72,6... | collective-permute-start | bytes 393224 | tf_op jit(solution)/shard_map/ppermute | solution.py:17
  583.5 13.6 %collective-permute-start.29 = (bf16[256,2,128]{2,0,1:T(8,128)(2,1)S(1)}, bf16[256,2,128]{2,0,1:T(8,128)(2,1)S(1)}, u32[]{:S(2)}, u32[]{:S(2)}) collective-permute-start(bf16[256,2,128]{2,0,1:T(8,128)(2,1)S(1)} %get-tuple-element.2065), channel_id=1, source_target_pairs={{16,0},{24,8},{32,16},{40,24},{48,32},{56,40},{64,48},{72,56},{80,... | collective-permute-start | bytes 393224 | tf_op jit(solution)/shard_map/ppermute | solution.py:17
  586.2 23.6 %collective-permute-start.30 = (bf16[256,2,128]{2,0,1:T(8,128)(2,1)S(1)}, bf16[256,2,128]{2,0,1:T(8,128)(2,1)S(1)}, u32[]{:S(2)}, u32[]{:S(2)}) collective-permute-start(bf16[256,2,128]{2,0,1:T(8,128)(2,1)S(1)} %get-tuple-element.2064), channel_id=1, source_target_pairs={{24,0},{32,8},{40,16},{48,24},{56,32},{64,40},{72,48},{80,56},{88,... | collective-permute-start | bytes 393224 | tf_op jit(solution)/shard_map/ppermute | solution.py:17
  593.4 16.4 %collective-permute-start.31 = (bf16[256,2,128]{2,0,1:T(8,128)(2,1)S(1)}, bf16[256,2,128]{2,0,1:T(8,128)(2,1)S(1)}, u32[]{:S(2)}, u32[]{:S(2)}) collective-permute-start(bf16[256,2,128]{2,0,1:T(8,128)(2,1)S(1)} %get-tuple-element.2063), channel_id=1, source_target_pairs={{32,0},{40,8},{48,16},{56,24},{64,32},{72,40},{80,48},{88,56},{96,... | collective-permute-start | bytes 393224 | tf_op jit(solution)/shard_map/ppermute | solution.py:17
  (33 other events, 133.6 us)
